TPU v7x, 512 devices: a whole 4x8x8 slice. The times are simulated.
512 devices in a mesh: dp: 32 (over z, y_lo, core), feat: 16 (over y_hi, x).
Axes of the slice: x: 4, y: 8 (y_hi: 4, y_lo: 2; y = y_hi * 2 + y_lo), z: 8, core: 2. Of those that a mesh axis runs over, the one named last changes fastest.
Arguments:
- tokens: bfloat16 [8192, 8192], P('dp', 'feat'), may hold values from -6 to 6
- up_left: bfloat16 [16, 512, 2048], P('feat', 'dp'), may hold values from -0.25 to 0.25
- up_right: bfloat16 [2048, 16, 16], P('feat'), may hold values from -1.5 to 1.5
- down_left: bfloat16 [16, 2048, 512], P('feat', 'dp'), may hold values from -0.125 to 0.125
- down_right: bfloat16 [512, 16, 16], P('feat'), may hold values from -1.5 to 1.5
- layer_grad: bfloat16 [8192, 8192], P('dp', 'feat'), may hold values from -6 to 6
Outputs:
- layer_out: bfloat16 [8192, 8192], P('dp', 'feat')
- grad_tokens: bfloat16 [8192, 8192], P('dp', 'feat')
- grad_up_left: float32 [16, 512, 2048], P('feat', 'dp')
- grad_up_right: float32 [2048, 16, 16], P('feat')
- grad_down_left: float32 [16, 2048, 512], P('feat', 'dp')
- grad_down_right: float32 [512, 16, 16], P('feat')
All inputs are finite; a program needn't handle non-finite values.
Results may differ from a plain program's by a relative error of at most 0.0067.
Values may be sent and summed in bfloat16 or wider, within the bound.
No kernel may reach another device: no remote copies, remote signals or barrier semaphores. Data moves between devices by JAX's collectives and lax.ppermute only.
A program may use at most 128 MiB of HBM per device.

v0:
```python
import jax
import jax.numpy as jnp
import numpy as np
from jax import lax
from jax.sharding import Mesh
from jax.sharding import PartitionSpec as P

TILE_UP = 128
TILE_DOWN = 32
DP_AXES = ("z", "ylo", "core")
FEAT_AXES = ("yhi", "x")


def split_mesh(mesh):
    n_dp = mesh.shape["dp"]
    n_feat = mesh.shape["feat"]
    sizes = (n_dp // 4, 2, 2, n_feat // 4, 4)
    devices = np.asarray(mesh.devices).reshape(sizes)
    return Mesh(devices, DP_AXES + FEAT_AXES)


def exchange(wired):
    rows, feat_count, piece = wired.shape
    n_x = lax.axis_size("x")
    n_y = feat_count // n_x
    shaped = wired.reshape(rows, n_y, n_x, piece)
    shaped = lax.all_to_all(shaped, "x", 2, 2, tiled=True)
    shaped = lax.all_to_all(shaped, "yhi", 1, 1, tiled=True)
    return shaped.reshape(rows, feat_count, piece)


def dp_reduce_scatter(part, row_axis):
    shape = part.shape
    rows = shape[row_axis]
    n_z = lax.axis_size("z")
    split = shape[:row_axis] + (n_z, 2, 2, rows // (4 * n_z)) + shape[row_axis + 1 :]
    x = part.reshape(split)
    x = lax.psum_scatter(x, "core", scatter_dimension=row_axis + 2, tiled=True)
    x = lax.psum_scatter(x, "z", scatter_dimension=row_axis, tiled=True)
    x = lax.psum_scatter(x, "ylo", scatter_dimension=row_axis + 1, tiled=True)
    return x.reshape(shape[:row_axis] + (rows // (4 * n_z),) + shape[row_axis + 1 :])


def dp_all_gather(local, row_axis):
    shape = local.shape
    rows = shape[row_axis]
    x = local.reshape(shape[:row_axis] + (1, 1, 1, rows) + shape[row_axis + 1 :])
    x = lax.all_gather(x, "ylo", axis=row_axis + 1, tiled=True)
    x = lax.all_gather(x, "z", axis=row_axis, tiled=True)
    x = lax.all_gather(x, "core", axis=row_axis + 2, tiled=True)
    total = x.shape[row_axis] * x.shape[row_axis + 1] * x.shape[row_axis + 2] * rows
    return x.reshape(shape[:row_axis] + (total,) + shape[row_axis + 1 :])


def to_wire(blocks, feat_count):
    tok_rows, local_blocks, full_width = blocks.shape
    piece = full_width // feat_count
    shaped = blocks.reshape(tok_rows, local_blocks, feat_count, piece).transpose(0, 2, 1, 3)
    return shaped.reshape(tok_rows, feat_count, local_blocks * piece)


def from_wire(wired, local_blocks):
    tok_rows, feat_count, line_len = wired.shape
    piece = line_len // local_blocks
    shaped = wired.reshape(tok_rows, feat_count, local_blocks, piece).transpose(0, 2, 1, 3)
    return shaped.reshape(tok_rows, local_blocks, feat_count * piece)


def on_device(tokens, up_left, up_right, down_left, down_right, layer_grad):
    tok_rows = tokens.shape[0]
    local_blocks = up_left.shape[0]
    hidden_width = up_left.shape[2]
    block_width = down_left.shape[2]
    blocks_all = up_right.shape[1]
    group_up = up_right.shape[0]
    group_down = down_right.shape[0]
    feat_count = lax.axis_size("yhi") * lax.axis_size("x")
    n_dp = lax.axis_size("z") * lax.axis_size("ylo") * lax.axis_size("core")
    grad_scale = float(tok_rows * n_dp) ** (-0.5)
    tiles_up = group_up // TILE_UP
    tiles_down = group_down // TILE_DOWN
    up_full = dp_all_gather(up_left, 1)
    token_blocks = tokens.reshape(tok_rows, local_blocks, block_width)
    up_inner = jnp.einsum(
        "tbi,big->tbg", token_blocks, up_full, preferred_element_type=jnp.float32
    ).astype(jnp.bfloat16)
    up_mixed = exchange(to_wire(up_inner, feat_count))
    preact = jnp.einsum("tjg,gjk->tkg", up_mixed, up_right, preferred_element_type=jnp.float32)
    sigmoid_val = jax.nn.sigmoid(preact)
    activated = (
        (preact * sigmoid_val)
        .reshape(tok_rows, blocks_all, tiles_up, TILE_UP)
        .transpose(0, 2, 1, 3)
    )
    hidden = activated.reshape(tok_rows, local_blocks, hidden_width).astype(jnp.bfloat16)
    down_full = dp_all_gather(down_left, 1)
    down_inner = jnp.einsum(
        "tbh,bhc->tbc", hidden, down_full, preferred_element_type=jnp.float32
    ).astype(jnp.bfloat16)
    down_mixed = exchange(to_wire(down_inner, feat_count)).reshape(
        tok_rows, blocks_all * group_down
    )
    identity = jnp.eye(group_down, dtype=jnp.bfloat16).reshape(group_down, tiles_down, TILE_DOWN)
    mix_matrix = jnp.einsum(
        "cjk,cal->jcakl", down_right, identity, preferred_element_type=jnp.float32
    )
    mix_matrix = mix_matrix.astype(jnp.bfloat16).reshape(
        blocks_all * group_down, blocks_all * group_down
    )
    layer_out = jnp.dot(down_mixed, mix_matrix, preferred_element_type=jnp.float32).astype(
        jnp.bfloat16
    )
    grad_down_mixed = lax.dot_general(
        layer_grad, mix_matrix, (((1,), (1,)), ((), ())), preferred_element_type=jnp.float32
    ).astype(jnp.bfloat16)
    grad_by_group = layer_grad.reshape(tok_rows, tiles_down, blocks_all, TILE_DOWN).transpose(
        0, 2, 1, 3
    )
    grad_by_group = grad_by_group.reshape(tok_rows, blocks_all, group_down)
    right_down_term = (
        jnp.einsum(
            "tjc,tkc->cjk",
            down_mixed.reshape(tok_rows, blocks_all, group_down),
            grad_by_group,
            preferred_element_type=jnp.float32,
        )
        * grad_scale
    )
    grad_down_inner = from_wire(
        exchange(grad_down_mixed.reshape(tok_rows, feat_count, local_blocks * group_down)),
        local_blocks,
    )
    grad_down_left = dp_reduce_scatter(
        jnp.einsum("tbh,tbc->hbc", hidden, grad_down_inner, preferred_element_type=jnp.float32)
        * grad_scale,
        0,
    ).transpose(1, 0, 2)
    grad_hidden = jnp.einsum(
        "tbc,bhc->tbh", grad_down_inner, down_full, preferred_element_type=jnp.float32
    )
    grad_hidden = grad_hidden.reshape(tok_rows, tiles_up, blocks_all, TILE_UP).transpose(0, 2, 1, 3)
    grad_hidden = grad_hidden.reshape(tok_rows, blocks_all, group_up)
    grad_preact = (grad_hidden * sigmoid_val * (1.0 + preact * (1.0 - sigmoid_val))).astype(
        jnp.bfloat16
    )
    grad_up_mixed = jnp.einsum(
        "tkg,gjk->tjg", grad_preact, up_right, preferred_element_type=jnp.float32
    ).astype(jnp.bfloat16)
    right_up_term = (
        jnp.einsum("tjg,tkg->gjk", up_mixed, grad_preact, preferred_element_type=jnp.float32)
        * grad_scale
    )
    grad_up_inner = from_wire(exchange(grad_up_mixed), local_blocks)
    grad_tokens = jnp.einsum(
        "tbg,big->tbi", grad_up_inner, up_full, preferred_element_type=jnp.float32
    ).astype(jnp.bfloat16)
    grad_tokens = grad_tokens.reshape(tok_rows, local_blocks * block_width)
    grad_up_left = dp_reduce_scatter(
        jnp.einsum("tbi,tbg->ibg", token_blocks, grad_up_inner, preferred_element_type=jnp.float32)
        * grad_scale,
        0,
    ).transpose(1, 0, 2)
    rights = jnp.concatenate([right_up_term, right_down_term], axis=0)
    rights = lax.psum(rights, DP_AXES)
    grad_up_right = rights[:group_up]
    grad_down_right = rights[group_up:]
    return (layer_out, grad_tokens, grad_up_left, grad_up_right, grad_down_left, grad_down_right)


def solution(mesh):
    fine = split_mesh(mesh)
    row = P(DP_AXES, FEAT_AXES)
    weight = P(FEAT_AXES, DP_AXES, None)
    mixer = P(FEAT_AXES, None, None)
    return jax.shard_map(
        on_device,
        mesh=fine,
        in_specs=(row, weight, mixer, weight, mixer, row),
        out_specs=(row, row, weight, mixer, weight, mixer),
        check_vma=False,
    )
```

profile of v0, /device:TPU:1, one launch (start us, length us, event | category | flops | bytes accessed | tf_op | source)
XLA Modules:
  0.0 650.3 jit_solution(2913419054008153790)
XLA Ops:
  7.2 6.3 all-gather
  13.6 42.4 %all-gather.13.cloned.1.call-done = bf16[16,16,2048]{2,1,0:T(8,128)(2,1)} async-done(((bf16[2,16,2048]{2,1,0:T(8,128)(2,1)}), bf16[16,16,2048]{2,1,0:T(8,128)(2,1)}) %all-gather.13.cloned.1.call-update) | async-done | bytes 1048592 | tf_op jit(solution)/shard_map/all_gather | solution.py:49
  56.1 5.3 all-gather.2
  66.9 4.0 all-to-all-start.4
  70.8 10.1 %all-gather.9.cloned.1.call-done = bf16[1,8,2,2,16,2048]{5,4,3,2,1,0:T(8,128)(2,1)} async-done(((bf16[1,8,2,1,16,2048]{5,4,3,2,1,0:T(8,128)(2,1)}), bf16[1,8,2,2,16,2048]{5,4,3,2,1,0:T(8,128)(2,1)}) %all-gather.9.cloned.1.call-update) | async-done | bytes 2097168 | tf_op jit(solution)/shard_map/all_gather | solution.py:50
  80.9 2.3 convolution_convert_fusion
  84.4 3.5 all-to-all-start
  87.9 32.6 %all-gather.15.cloned.1.call-done = bf16[16,64,512]{2,1,0:T(8,128)(2,1)} async-done(((bf16[2,64,512]{2,1,0:T(8,128)(2,1)}), bf16[16,64,512]{2,1,0:T(8,128)(2,1)}) %all-gather.15.cloned.1.call-update) | async-done | bytes 1048592 | tf_op jit(solution)/shard_map/all_gather | solution.py:49
  121.3 6.5 all-to-all-start.5
  128.8 6.9 %all-to-all-done.5 = bf16[256,4,4,32]{0,3,2,1:T(8,128)(2,1)S(1)} async-done(((bf16[256,4,4,32]{0,3,2,1:T(8,128)(2,1)}), bf16[256,4,4,32]{0,3,2,1:T(8,128)(2,1)S(1)}, u32[]{:S(2)}, u32[]{:S(2)}) %all-to-all-start.5) | async-done | bytes 262176 | tf_op jit(solution)/shard_map/all_to_all | solution.py:28
  135.7 4.3 all-to-all-start.1
  141.2 4.1 all-gather.11.cloned.1.call-done
  147.6 18.1 %all-to-all-done.1 = bf16[256,4,4,128]{0,3,2,1:T(8,128)(2,1)} async-done(((bf16[256,4,4,128]{0,3,2,1:T(8,128)(2,1)}), bf16[256,4,4,128]{0,3,2,1:T(8,128)(2,1)}, u32[]{:S(2)}, u32[]{:S(2)}) %all-to-all-start.1) | async-done | bytes 1048608 | tf_op jit(solution)/shard_map/all_to_all | solution.py:28
  165.8 4.5 fusion.7
  172.3 15.0 %all_to_all.40 = bf16[256,4,4,128]{0,3,1,2:T(8,128)(2,1)S(1)} all-to-all(bf16[256,4,4,128]{0,3,1,2:T(8,128)(2,1)S(1)} %copy.95), channel_id=1, replica_groups=mesh['z'=8,'ylo'=2,'core'=2,'yhi'=4,'x'=4] {'x'}, dimensions={2} | all-to-all | bytes 2097152 | tf_op jit(solution)/shard_map/all_to_all | solution.py:27
  188.4 6.5 %all-to-all-start.7 = ((bf16[256,4,4,128]{0,3,2,1:T(8,128)(2,1)}), bf16[256,4,4,128]{0,3,2,1:T(8,128)(2,1)S(1)}, u32[]{:S(2)}, u32[]{:S(2)}) async-start(bf16[256,4,4,128]{0,3,2,1:T(8,128)(2,1)} %copy.96), calls=%async_computation.7 | async-start | bytes 2097152 | tf_op jit(solution)/shard_map/all_to_all | solution.py:28
  196.3 2.7 multiply_bitcast_fusion
  199.0 5.4 copy.103
  204.5 10.2 %all-to-all-done.7 = bf16[256,4,4,128]{0,3,2,1:T(8,128)(2,1)S(1)} async-done(((bf16[256,4,4,128]{0,3,2,1:T(8,128)(2,1)}), bf16[256,4,4,128]{0,3,2,1:T(8,128)(2,1)S(1)}, u32[]{:S(2)}, u32[]{:S(2)}) %all-to-all-start.7) | async-done | bytes 1048608 | tf_op jit(solution)/shard_map/all_to_all | solution.py:28
  214.7 2.7 convolution_multiply_fusion
  218.7 53.0 %all-reduce.8.cloned.1.call-done = (f32[8,2,2,16,1,2048]{5,3,4,2,1,0:T(8,128)}, f32[8,2,2,64,1,512]{5,3,2,1,0,4:T(8,128)}) async-done(((f32[8,2,2,16,1,2048]{5,3,4,2,1,0:T(8,128)}, f32[8,2,2,64,1,512]{5,3,2,1,0,4:T(8,128)}), (f32[8,2,2,16,1,2048]{5,3,4,2,1,0:T(8,128)}, f32[8,2,2,64,1,512]{5,3,2,1,0,4:T(8,128)})) %all-reduce.8.cloned.1.call-update) | async-done | bytes 8388624
  271.7 3.9 constant_dynamic-slice_fusion
  275.6 3.9 constant_dynamic-slice_fusion.1
  283.2 9.2 %all_to_all.41 = bf16[256,4,4,32]{0,3,1,2:T(8,128)(2,1)S(1)} all-to-all(bf16[256,4,4,32]{0,3,1,2:T(8,128)(2,1)S(1)} %copy.87), channel_id=1, replica_groups=mesh['z'=8,'ylo'=2,'core'=2,'yhi'=4,'x'=4] {'x'}, dimensions={2} | all-to-all | bytes 524288 | tf_op jit(solution)/shard_map/all_to_all | solution.py:27
  293.1 6.5 all-to-all-start.3
  302.9 5.1 all-to-all-done.3
  309.3 7.6 %reduce-scatter.13.cloned.1.call-done = f32[1,2,1,64,1,512]{5,3,2,1,0,4:T(8,128)} async-done(((f32[8,2,1,64,1,512]{5,3,2,1,0,4:T(8,128)}), f32[1,2,1,64,1,512]{5,3,2,1,0,4:T(8,128)}) %reduce-scatter.13.cloned.1.call-update) | async-done | bytes 262160 | tf_op jit(solution)/shard_map/reduce_scatter | solution.py:39
  317.0 46.2 %reduce-scatter.9.cloned.1.call-done = f32[1,2,1,16,1,2048]{5,3,4,2,1,0:T(8,128)} async-done(((f32[8,2,1,16,1,2048]{5,3,4,2,1,0:T(8,128)}), f32[1,2,1,16,1,2048]{5,3,4,2,1,0:T(8,128)}) %reduce-scatter.9.cloned.1.call-update) | async-done | bytes 262160 | tf_op jit(solution)/shard_map/reduce_scatter | solution.py:39
  364.3 233.1 %all-reduce.6.cloned.1.call-done = f32[160,16,16]{0,2,1:T(8,128)} async-done(((f32[160,16,16]{0,2,1:T(8,128)}), f32[160,16,16]{0,2,1:T(8,128)}) %all-reduce.6.cloned.1.call-update) | async-done | bytes 163856 | tf_op jit(solution)/shard_map/psum | solution.py:164
  600.6 3.0 convolution_convert_fusion.2
  603.6 16.7 %reduce-scatter.15.cloned.1.call-done = f32[1,1,1,64,1,512]{5,3,2,1,0,4:T(8,128)} async-done(((f32[1,2,1,64,1,512]{5,3,2,1,0,4:T(8,128)}), f32[1,1,1,64,1,512]{5,3,2,1,0,4:T(8,128)}) %reduce-scatter.15.cloned.1.call-update) | async-done | bytes 131088 | tf_op jit(solution)/shard_map/reduce_scatter | solution.py:40
  620.3 23.2 %reduce-scatter.11.cloned.1.call-done = f32[1,1,1,16,1,2048]{5,3,4,2,1,0:T(8,128)} async-done(((f32[1,2,1,16,1,2048]{5,3,4,2,1,0:T(8,128)}), f32[1,1,1,16,1,2048]{5,3,4,2,1,0:T(8,128)}) %reduce-scatter.11.cloned.1.call-update) | async-done | bytes 131088 | tf_op jit(solution)/shard_map/reduce_scatter | solution.py:40
  (76 shorter events, 31.2 us)
Async XLA Ops:
  7.2 73.8 %copy-start = (bf16[256,512]{1,0:T(8,128)(2,1)S(1)}, bf16[256,512]{1,0:T(8,128)(2,1)}, u32[]{:S(2)}) copy-start(bf16[256,512]{1,0:T(8,128)(2,1)} %param.6) | copy-start | bytes 786436
  7.2 48.8 %all-gather.13.cloned.1.call-start = ((), (), s32[]{:S(2)}) async-start(), calls=%async_computation.19 | async-start | bytes 1179648 | tf_op jit(solution)/shard_map/all_gather | solution.py:49
  13.6 67.3 %all-gather.9.cloned.1.call-start = ((), (), s32[]{:S(2)}) async-start(), calls=%async_computation.12 | async-start | bytes 3145728 | tf_op jit(solution)/shard_map/all_gather | solution.py:50
  56.0 64.5 %all-gather.15.cloned.1.call-start = ((), (), s32[]{:S(2)}) async-start(), calls=%async_computation.20 | async-start | bytes 1179648 | tf_op jit(solution)/shard_map/all_gather | solution.py:49
  62.3 3.5 copy-start.9
  66.9 17.5 %all-to-all-start.4 = ((bf16[256,4,4,32]{0,3,1,2:T(8,128)(2,1)}), bf16[256,4,4,32]{0,3,1,2:T(8,128)(2,1)S(1)}, u32[]{:S(2)}, u32[]{:S(2)}) async-start(bf16[256,4,4,32]{0,3,1,2:T(8,128)(2,1)} %copy.90), calls=%async_computation.4 | async-start | bytes 524288 | tf_op jit(solution)/shard_map/all_to_all | solution.py:27
  84.4 37.0 %all-to-all-start = ((bf16[256,4,4,128]{0,3,1,2:T(8,128)(2,1)}), bf16[256,4,4,128]{0,3,1,2:T(8,128)(2,1)S(1)}, u32[]{:S(2)}, u32[]{:S(2)}) async-start(bf16[256,4,4,128]{0,3,1,2:T(8,128)(2,1)} %copy.81), calls=%async_computation | async-start | bytes 2097152 | tf_op jit(solution)/shard_map/all_to_all | solution.py:27
  87.9 57.4 %all-gather.11.cloned.1.call-start = ((), (), s32[]{:S(2)}) async-start(), calls=%async_computation.13 | async-start | bytes 3145728 | tf_op jit(solution)/shard_map/all_gather | solution.py:50
  121.3 14.4 %all-to-all-start.5 = ((bf16[256,4,4,32]{0,3,2,1:T(8,128)(2,1)}), bf16[256,4,4,32]{0,3,2,1:T(8,128)(2,1)S(1)}, u32[]{:S(2)}, u32[]{:S(2)}) async-start(bf16[256,4,4,32]{0,3,2,1:T(8,128)(2,1)} %copy.91), calls=%async_computation.5 | async-start | bytes 524288 | tf_op jit(solution)/shard_map/all_to_all | solution.py:28
  127.8 12.2 %copy-start.11 = (bf16[128,16,16]{0,2,1:T(8,128)(2,1)S(1)}, bf16[128,16,16]{0,2,1:T(8,128)(2,1)}, u32[]{:S(2)}) copy-start(bf16[128,16,16]{0,2,1:T(8,128)(2,1)} %param.8) | copy-start | bytes 196612
  135.7 30.0 %all-to-all-start.1 = ((bf16[256,4,4,128]{0,3,2,1:T(8,128)(2,1)}), bf16[256,4,4,128]{0,3,2,1:T(8,128)(2,1)}, u32[]{:S(2)}, u32[]{:S(2)}) async-start(bf16[256,4,4,128]{0,3,2,1:T(8,128)(2,1)} %copy.82), calls=%async_computation.1 | async-start | bytes 2097152 | tf_op jit(solution)/shard_map/all_to_all | solution.py:28
  165.7 5.5 copy-start.7
  170.2 1.0 copy-start.2
  187.3 7.6 %copy-start.8 = (bf16[256,16,128]{0,1,2:T(8,128)(2,1)S(1)}, bf16[256,16,128]{0,1,2:T(8,128)(2,1)}, u32[]{:S(2)}) copy-start(bf16[256,16,128]{0,1,2:T(8,128)(2,1)} %get-tuple-element.21) | copy-start | bytes 3145732
  188.4 26.3 %all-to-all-start.7 = ((bf16[256,4,4,128]{0,3,2,1:T(8,128)(2,1)}), bf16[256,4,4,128]{0,3,2,1:T(8,128)(2,1)S(1)}, u32[]{:S(2)}, u32[]{:S(2)}) async-start(bf16[256,4,4,128]{0,3,2,1:T(8,128)(2,1)} %copy.96), calls=%async_computation.7 | async-start | bytes 2097152 | tf_op jit(solution)/shard_map/all_to_all | solution.py:28
  194.9 76.8 %all-reduce.8.cloned.1.call-start = ((), (), s32[]{:S(2)}) async-start(), calls=%async_computation.21 | async-start | bytes 16777216
  195.2 1.1 copy-start.6
  214.7 2.7 copy-start.4
  217.4 99.6 %reduce-scatter.13.cloned.1.call-start = ((), (), s32[]{:S(2)}) async-start(), calls=%async_computation.17 | async-start | bytes 2359296 | tf_op jit(solution)/shard_map/reduce_scatter | solution.py:39
  275.6 87.7 %reduce-scatter.9.cloned.1.call-start = ((), (), s32[]{:S(2)}) async-start(), calls=%async_computation.14 | async-start | bytes 2359296 | tf_op jit(solution)/shard_map/reduce_scatter | solution.py:39
  279.5 1.6 copy-start.1
  283.1 17.4 %copy-start.3 = (bf16[256,16,128]{0,1,2:T(8,128)(2,1)S(1)}, bf16[256,16,128]{0,1,2:T(8,128)(2,1)}, u32[]{:S(2)}) copy-start(bf16[256,16,128]{0,1,2:T(8,128)(2,1)} %copy-done.2) | copy-start | bytes 3145732
  293.1 14.8 %all-to-all-start.3 = ((bf16[256,4,4,32]{0,3,2,1:T(8,128)(2,1)}), bf16[256,4,4,32]{0,3,2,1:T(8,128)(2,1)S(1)}, u32[]{:S(2)}, u32[]{:S(2)}) async-start(bf16[256,4,4,32]{0,3,2,1:T(8,128)(2,1)} %copy.88), calls=%async_computation.3 | async-start | bytes 524288 | tf_op jit(solution)/shard_map/all_to_all | solution.py:28
  299.6 297.9 %all-reduce.6.cloned.1.call-start = ((), (), s32[]{:S(2)}) async-start(), calls=%async_computation.16 | async-start | bytes 524288 | tf_op jit(solution)/shard_map/psum | solution.py:164
  300.4 7.5 %copy-start.10 = (bf16[256,512]{0,1:T(8,128)(2,1)S(1)}, bf16[256,512]{0,1:T(8,128)(2,1)}, u32[]{:S(2)}) copy-start(bf16[256,512]{0,1:T(8,128)(2,1)} %copy.99) | copy-start | bytes 786436
  302.9 297.7 %copy-start.5 = (bf16[256,4,4,128]{0,3,2,1:T(8,128)(2,1)S(1)}, bf16[256,4,4,128]{0,3,2,1:T(8,128)(2,1)}, u32[]{:S(2)}) copy-start(bf16[256,4,4,128]{0,3,2,1:T(8,128)(2,1)} %copy-done.4) | copy-start | bytes 3145732
  309.3 311.0 %reduce-scatter.15.cloned.1.call-start = ((), (), s32[]{:S(2)}) async-start(), calls=%async_computation.18 | async-start | bytes 393216 | tf_op jit(solution)/shard_map/reduce_scatter | solution.py:40
  317.0 326.5 %reduce-scatter.11.cloned.1.call-start = ((), (), s32[]{:S(2)}) async-start(), calls=%async_computation.15 | async-start | bytes 393216 | tf_op jit(solution)/shard_map/reduce_scatter | solution.py:40
Sparse Core Ops, SparseCore 0:
  13.7 42.2 all-gather.12
  58.1 22.8 all-gather.8
  83.0 37.5 all-gather.14
  122.5 22.7 all-gather.10
  217.5 54.1 all-reduce.7
  275.7 41.1 reduce-scatter.12
  319.8 43.4 reduce-scatter.8
  366.7 230.6 all-reduce.5
  601.0 19.2 reduce-scatter.14
  623.5 19.9 reduce-scatter.10
where the time goes:
time: 652 us; the launch traced here: 650 us
  waiting for transfers between devices  509 us (78%)
  blocking collectives  35.8 us (5%)
  local copies, waits for them, and re-layouts  33.3 us (5%)
  starting transfers between devices  31.5 us (5%)
  matrix products  23.7 us (4%)
  between operations  14.3 us (2%)
    psum x1, waiting for transfers between devices, on_device(): rights = lax.psum(rights, DP_AXES)  233 us
    all_gather x2, waiting for transfers between devices, dp_all_gather(): x = lax.all_gather(x, 'z', axis=row_axis, tiled=True)  75 us
    reduce_scatter x2, waiting for transfers between devices, dp_reduce_scatter(): x = lax.psum_scatter(x, 'z', scatter_dimension=row_axis, tiled=True)  53.9 us
    unnamed x11, waiting for transfers between devices  53.1 us
    all_to_all x4, waiting for transfers between devices, exchange(): shaped = lax.all_to_all(shaped, 'yhi', 1, 1, tiled=True)  40.3 us
    reduce_scatter x2, waiting for transfers between devices, dp_reduce_scatter(): x = lax.psum_scatter(x, 'ylo', scatter_dimension=row_axis + 1, tiled=True)  39.8 us
    all_to_all x2, blocking collectives, exchange(): shaped = lax.all_to_all(shaped, 'x', 2, 2, tiled=True)  24.2 us
    all_to_all x4, starting transfers between devices, exchange(): shaped = lax.all_to_all(shaped, 'yhi', 1, 1, tiled=True)  23.7 us
  transfers between devices with their start and end apart: 16, of which 14 were waited for; matrix products, arithmetic and copies ran while one was open for 7% of the time, Pallas kernels for 0%

commit v1 on v0

--- a/solution.py
+++ b/solution.py
@@ -161,7 +161,7 @@
         0,
     ).transpose(1, 0, 2)
     rights = jnp.concatenate([right_up_term, right_down_term], axis=0)
-    rights = lax.psum(rights, DP_AXES)
+    rights = lax.psum(lax.psum(rights, "z"), ("ylo", "core"))
     grad_up_right = rights[:group_up]
     grad_down_right = rights[group_up:]
     return (layer_out, grad_tokens, grad_up_left, grad_up_right, grad_down_left, grad_down_right)

time: 652 us -> 549 us (0.84)
  waiting for transfers between devices: 509 us -> 410 us
    psum x1 -> x2, waiting for transfers between devices: 233 us -> 120 us  [on_device(): rights = lax.psum(lax.psum(rights, 'z'), ('ylo', 'core'))]
    reduce_scatter x2, waiting for transfers between devices: 53.9 us -> 93.8 us  [dp_reduce_scatter(): x = lax.psum_scatter(x, 'z', scatter_dimension=row_axis, tiled=True)]
    unnamed x11 -> x12, waiting for transfers between devices: 53.1 us -> 29 us
  transfers between devices with their start and end apart: 16 -> 17, of which waited for: 14 -> 15; matrix products, arithmetic and copies ran while one was open for 7% -> 8% of each run, Pallas kernels for 0% -> 0%
where the time goes in v1:
time: 549 us; the launch traced here: 548 us
  waiting for transfers between devices  410 us (75%)
  blocking collectives  34.7 us (6%)
  local copies, waits for them, and re-layouts  33.3 us (6%)
  starting transfers between devices  29.1 us (5%)
  matrix products  24 us (4%)
  between operations  14.1 us (3%)
    psum x2, waiting for transfers between devices, on_device(): rights = lax.psum(lax.psum(rights, 'z'), ('ylo', 'core'))  120 us
    reduce_scatter x2, waiting for transfers between devices, dp_reduce_scatter(): x = lax.psum_scatter(x, 'z', scatter_dimension=row_axis, tiled=True)  93.8 us
    all_gather x2, waiting for transfers between devices, dp_all_gather(): x = lax.all_gather(x, 'z', axis=row_axis, tiled=True)  75 us
    reduce_scatter x2, waiting for transfers between devices, dp_reduce_scatter(): x = lax.psum_scatter(x, 'ylo', scatter_dimension=row_axis + 1, tiled=True)  40 us
    all_to_all x4, waiting for transfers between devices, exchange(): shaped = lax.all_to_all(shaped, 'yhi', 1, 1, tiled=True)  38.2 us
    unnamed x12, waiting for transfers between devices  29 us
    all_to_all x2, blocking collectives, exchange(): shaped = lax.all_to_all(shaped, 'x', 2, 2, tiled=True)  23.1 us
    all_to_all x4, starting transfers between devices, exchange(): shaped = lax.all_to_all(shaped, 'yhi', 1, 1, tiled=True)  21.3 us
  transfers between devices with their start and end apart: 17, of which 15 were waited for; matrix products, arithmetic and copies ran while one was open for 8% of the time, Pallas kernels for 0%

profile of v1, /device:TPU:1, one launch (start us, length us, event | category | flops | bytes accessed | tf_op | source)
XLA Modules:
  0.0 547.8 jit_solution(15136318549710244127)
XLA Ops:
  7.2 6.3 %all-gather = bf16[2,16,2048]{2,1,0:T(8,128)(2,1)} all-gather(bf16[1,16,2048]{2,1,0:T(8,128)(2,1)} %param.7), channel_id=2, replica_groups=mesh['z'=8,'ylo'=2,'core'=2,'yhi'=4,'x'=4] {'ylo'}, dimensions={0}, use_global_device_ids=true | all-gather | bytes 196608 | tf_op jit(solution)/shard_map/all_gather | solution.py:48
  13.6 42.4 %all-gather.13.cloned.1.call-done = bf16[16,16,2048]{2,1,0:T(8,128)(2,1)} async-done(((bf16[2,16,2048]{2,1,0:T(8,128)(2,1)}), bf16[16,16,2048]{2,1,0:T(8,128)(2,1)}) %all-gather.13.cloned.1.call-update) | async-done | bytes 1048592 | tf_op jit(solution)/shard_map/all_gather | solution.py:49
  56.1 5.3 all-gather.2
  66.9 4.0 all-to-all-start.4
  70.8 10.1 %all-gather.9.cloned.1.call-done = bf16[1,8,2,2,16,2048]{5,4,3,2,1,0:T(8,128)(2,1)} async-done(((bf16[1,8,2,1,16,2048]{5,4,3,2,1,0:T(8,128)(2,1)}), bf16[1,8,2,2,16,2048]{5,4,3,2,1,0:T(8,128)(2,1)}) %all-gather.9.cloned.1.call-update) | async-done | bytes 2097168 | tf_op jit(solution)/shard_map/all_gather | solution.py:50
  84.4 3.5 all-to-all-start
  87.9 32.6 %all-gather.15.cloned.1.call-done = bf16[16,64,512]{2,1,0:T(8,128)(2,1)} async-done(((bf16[2,64,512]{2,1,0:T(8,128)(2,1)}), bf16[16,64,512]{2,1,0:T(8,128)(2,1)}) %all-gather.15.cloned.1.call-update) | async-done | bytes 1048592 | tf_op jit(solution)/shard_map/all_gather | solution.py:49
  121.3 6.5 %all-to-all-start.5 = ((bf16[256,4,4,32]{0,3,2,1:T(8,128)(2,1)}), bf16[256,4,4,32]{0,3,2,1:T(8,128)(2,1)S(1)}, u32[]{:S(2)}, u32[]{:S(2)}) async-start(bf16[256,4,4,32]{0,3,2,1:T(8,128)(2,1)} %copy.91), calls=%async_computation.5 | async-start | bytes 524288 | tf_op jit(solution)/shard_map/all_to_all | solution.py:28
  128.8 6.9 %all-to-all-done.5 = bf16[256,4,4,32]{0,3,2,1:T(8,128)(2,1)S(1)} async-done(((bf16[256,4,4,32]{0,3,2,1:T(8,128)(2,1)}), bf16[256,4,4,32]{0,3,2,1:T(8,128)(2,1)S(1)}, u32[]{:S(2)}, u32[]{:S(2)}) %all-to-all-start.5) | async-done | bytes 262176 | tf_op jit(solution)/shard_map/all_to_all | solution.py:28
  135.7 4.2 all-to-all-start.1
  141.1 4.2 all-gather.11.cloned.1.call-done
  147.6 18.1 %all-to-all-done.1 = bf16[256,4,4,128]{0,3,2,1:T(8,128)(2,1)} async-done(((bf16[256,4,4,128]{0,3,2,1:T(8,128)(2,1)}), bf16[256,4,4,128]{0,3,2,1:T(8,128)(2,1)}, u32[]{:S(2)}, u32[]{:S(2)}) %all-to-all-start.1) | async-done | bytes 1048608 | tf_op jit(solution)/shard_map/all_to_all | solution.py:28
  165.7 4.5 fusion.7
  172.2 15.0 %all_to_all.40 = bf16[256,4,4,128]{0,3,1,2:T(8,128)(2,1)S(1)} all-to-all(bf16[256,4,4,128]{0,3,1,2:T(8,128)(2,1)S(1)} %copy.95), channel_id=1, replica_groups=mesh['z'=8,'ylo'=2,'core'=2,'yhi'=4,'x'=4] {'x'}, dimensions={2} | all-to-all | bytes 2097152 | tf_op jit(solution)/shard_map/all_to_all | solution.py:27
  188.3 6.5 %all-to-all-start.7 = ((bf16[256,4,4,128]{0,3,2,1:T(8,128)(2,1)}), bf16[256,4,4,128]{0,3,2,1:T(8,128)(2,1)S(1)}, u32[]{:S(2)}, u32[]{:S(2)}) async-start(bf16[256,4,4,128]{0,3,2,1:T(8,128)(2,1)} %copy.96), calls=%async_computation.7 | async-start | bytes 2097152 | tf_op jit(solution)/shard_map/all_to_all | solution.py:28
  196.3 2.7 multiply_bitcast_fusion
  199.0 5.4 copy.103
  204.5 10.1 %all-to-all-done.7 = bf16[256,4,4,128]{0,3,2,1:T(8,128)(2,1)S(1)} async-done(((bf16[256,4,4,128]{0,3,2,1:T(8,128)(2,1)}), bf16[256,4,4,128]{0,3,2,1:T(8,128)(2,1)S(1)}, u32[]{:S(2)}, u32[]{:S(2)}) %all-to-all-start.7) | async-done | bytes 1048608 | tf_op jit(solution)/shard_map/all_to_all | solution.py:28
  214.6 2.7 convolution_multiply_fusion
  221.0 8.0 %all_to_all.41 = bf16[256,4,4,32]{0,3,1,2:T(8,128)(2,1)S(1)} all-to-all(bf16[256,4,4,32]{0,3,1,2:T(8,128)(2,1)S(1)} %copy.87), channel_id=1, replica_groups=mesh['z'=8,'ylo'=2,'core'=2,'yhi'=4,'x'=4] {'x'}, dimensions={2} | all-to-all | bytes 524288 | tf_op jit(solution)/shard_map/all_to_all | solution.py:27
  229.8 4.1 all-to-all-start.3
  238.7 3.1 all-to-all-done.3
  243.1 28.8 %all-reduce.11.cloned.1.call-done = (f32[8,2,2,16,1,2048]{5,3,4,2,1,0:T(8,128)}, f32[8,2,2,64,1,512]{5,3,2,1,0,4:T(8,128)}) async-done(((f32[8,2,2,16,1,2048]{5,3,4,2,1,0:T(8,128)}, f32[8,2,2,64,1,512]{5,3,2,1,0,4:T(8,128)}), (f32[8,2,2,16,1,2048]{5,3,4,2,1,0:T(8,128)}, f32[8,2,2,64,1,512]{5,3,2,1,0,4:T(8,128)})) %all-reduce.11.cloned.1.call-update) | async-done | bytes 8388624
  272.0 3.9 constant_dynamic-slice_fusion
  275.9 3.9 constant_dynamic-slice_fusion.1
  279.9 68.8 %all-reduce.7.cloned.1.call-done = f32[160,16,16]{0,2,1:T(8,128)} async-done(((f32[160,16,16]{0,2,1:T(8,128)}), f32[160,16,16]{0,2,1:T(8,128)}) %all-reduce.7.cloned.1.call-update) | async-done | bytes 163856 | tf_op jit(solution)/shard_map/psum | solution.py:164
  348.7 47.0 %reduce-scatter.13.cloned.1.call-done = f32[1,2,1,64,1,512]{5,3,2,1,0,4:T(8,128)} async-done(((f32[8,2,1,64,1,512]{5,3,2,1,0,4:T(8,128)}), f32[1,2,1,64,1,512]{5,3,2,1,0,4:T(8,128)}) %reduce-scatter.13.cloned.1.call-update) | async-done | bytes 262160 | tf_op jit(solution)/shard_map/reduce_scatter | solution.py:39
  395.8 46.8 %reduce-scatter.9.cloned.1.call-done = f32[1,2,1,16,1,2048]{5,3,4,2,1,0:T(8,128)} async-done(((f32[8,2,1,16,1,2048]{5,3,4,2,1,0:T(8,128)}), f32[1,2,1,16,1,2048]{5,3,4,2,1,0:T(8,128)}) %reduce-scatter.9.cloned.1.call-update) | async-done | bytes 262160 | tf_op jit(solution)/shard_map/reduce_scatter | solution.py:39
  443.7 51.3 %all-reduce.9.cloned.1.call-done = f32[160,16,16]{0,2,1:T(8,128)} async-done(((f32[160,16,16]{0,2,1:T(8,128)}), f32[160,16,16]{0,2,1:T(8,128)}) %all-reduce.9.cloned.1.call-update) | async-done | bytes 163856 | tf_op jit(solution)/shard_map/psum | solution.py:164
  498.2 3.0 convolution_convert_fusion.2
  501.2 16.5 %reduce-scatter.15.cloned.1.call-done = f32[1,1,1,64,1,512]{5,3,2,1,0,4:T(8,128)} async-done(((f32[1,2,1,64,1,512]{5,3,2,1,0,4:T(8,128)}), f32[1,1,1,64,1,512]{5,3,2,1,0,4:T(8,128)}) %reduce-scatter.15.cloned.1.call-update) | async-done | bytes 131088 | tf_op jit(solution)/shard_map/reduce_scatter | solution.py:40
  517.7 23.6 %reduce-scatter.11.cloned.1.call-done = f32[1,1,1,16,1,2048]{5,3,4,2,1,0:T(8,128)} async-done(((f32[1,2,1,16,1,2048]{5,3,4,2,1,0:T(8,128)}), f32[1,1,1,16,1,2048]{5,3,4,2,1,0:T(8,128)}) %reduce-scatter.11.cloned.1.call-update) | async-done | bytes 131088 | tf_op jit(solution)/shard_map/reduce_scatter | solution.py:40
  (79 shorter events, 33.9 us)
Async XLA Ops:
  7.2 73.8 %copy-start = (bf16[256,512]{1,0:T(8,128)(2,1)S(1)}, bf16[256,512]{1,0:T(8,128)(2,1)}, u32[]{:S(2)}) copy-start(bf16[256,512]{1,0:T(8,128)(2,1)} %param.6) | copy-start | bytes 786436
  7.2 48.8 %all-gather.13.cloned.1.call-start = ((), (), s32[]{:S(2)}) async-start(), calls=%async_computation.20 | async-start | bytes 1179648 | tf_op jit(solution)/shard_map/all_gather | solution.py:49
  13.6 67.3 %all-gather.9.cloned.1.call-start = ((), (), s32[]{:S(2)}) async-start(), calls=%async_computation.12 | async-start | bytes 3145728 | tf_op jit(solution)/shard_map/all_gather | solution.py:50
  56.0 64.5 %all-gather.15.cloned.1.call-start = ((), (), s32[]{:S(2)}) async-start(), calls=%async_computation.21 | async-start | bytes 1179648 | tf_op jit(solution)/shard_map/all_gather | solution.py:49
  62.3 3.5 copy-start.9
  66.9 17.5 %all-to-all-start.4 = ((bf16[256,4,4,32]{0,3,1,2:T(8,128)(2,1)}), bf16[256,4,4,32]{0,3,1,2:T(8,128)(2,1)S(1)}, u32[]{:S(2)}, u32[]{:S(2)}) async-start(bf16[256,4,4,32]{0,3,1,2:T(8,128)(2,1)} %copy.90), calls=%async_computation.4 | async-start | bytes 524288 | tf_op jit(solution)/shard_map/all_to_all | solution.py:27
  84.4 36.9 %all-to-all-start = ((bf16[256,4,4,128]{0,3,1,2:T(8,128)(2,1)}), bf16[256,4,4,128]{0,3,1,2:T(8,128)(2,1)S(1)}, u32[]{:S(2)}, u32[]{:S(2)}) async-start(bf16[256,4,4,128]{0,3,1,2:T(8,128)(2,1)} %copy.81), calls=%async_computation | async-start | bytes 2097152 | tf_op jit(solution)/shard_map/all_to_all | solution.py:27
  87.9 57.4 %all-gather.11.cloned.1.call-start = ((), (), s32[]{:S(2)}) async-start(), calls=%async_computation.13 | async-start | bytes 3145728 | tf_op jit(solution)/shard_map/all_gather | solution.py:50
  121.3 14.4 %all-to-all-start.5 = ((bf16[256,4,4,32]{0,3,2,1:T(8,128)(2,1)}), bf16[256,4,4,32]{0,3,2,1:T(8,128)(2,1)S(1)}, u32[]{:S(2)}, u32[]{:S(2)}) async-start(bf16[256,4,4,32]{0,3,2,1:T(8,128)(2,1)} %copy.91), calls=%async_computation.5 | async-start | bytes 524288 | tf_op jit(solution)/shard_map/all_to_all | solution.py:28
  127.8 12.2 %copy-start.11 = (bf16[128,16,16]{0,2,1:T(8,128)(2,1)S(1)}, bf16[128,16,16]{0,2,1:T(8,128)(2,1)}, u32[]{:S(2)}) copy-start(bf16[128,16,16]{0,2,1:T(8,128)(2,1)} %param.8) | copy-start | bytes 196612
  135.7 30.0 %all-to-all-start.1 = ((bf16[256,4,4,128]{0,3,2,1:T(8,128)(2,1)}), bf16[256,4,4,128]{0,3,2,1:T(8,128)(2,1)}, u32[]{:S(2)}, u32[]{:S(2)}) async-start(bf16[256,4,4,128]{0,3,2,1:T(8,128)(2,1)} %copy.82), calls=%async_computation.1 | async-start | bytes 2097152 | tf_op jit(solution)/shard_map/all_to_all | solution.py:28
  165.7 5.5 copy-start.7
  170.2 1.0 copy-start.2
  187.2 7.6 %copy-start.8 = (bf16[256,16,128]{0,1,2:T(8,128)(2,1)S(1)}, bf16[256,16,128]{0,1,2:T(8,128)(2,1)}, u32[]{:S(2)}) copy-start(bf16[256,16,128]{0,1,2:T(8,128)(2,1)} %get-tuple-element.21) | copy-start | bytes 3145732
  188.3 26.3 %all-to-all-start.7 = ((bf16[256,4,4,128]{0,3,2,1:T(8,128)(2,1)}), bf16[256,4,4,128]{0,3,2,1:T(8,128)(2,1)S(1)}, u32[]{:S(2)}, u32[]{:S(2)}) async-start(bf16[256,4,4,128]{0,3,2,1:T(8,128)(2,1)} %copy.96), calls=%async_computation.7 | async-start | bytes 2097152 | tf_op jit(solution)/shard_map/all_to_all | solution.py:28
  194.8 77.1 %all-reduce.11.cloned.1.call-start = ((), (), s32[]{:S(2)}) async-start(), calls=%async_computation.22 | async-start | bytes 16777216
  195.2 1.1 copy-start.6
  214.6 2.7 copy-start.4
  217.3 1.6 copy-start.1
  220.8 15.1 %copy-start.3 = (bf16[256,16,128]{0,1,2:T(8,128)(2,1)S(1)}, bf16[256,16,128]{0,1,2:T(8,128)(2,1)}, u32[]{:S(2)}) copy-start(bf16[256,16,128]{0,1,2:T(8,128)(2,1)} %copy-done.2) | copy-start | bytes 3145732
  229.8 12.0 %all-to-all-start.3 = ((bf16[256,4,4,32]{0,3,2,1:T(8,128)(2,1)}), bf16[256,4,4,32]{0,3,2,1:T(8,128)(2,1)S(1)}, u32[]{:S(2)}, u32[]{:S(2)}) async-start(bf16[256,4,4,32]{0,3,2,1:T(8,128)(2,1)} %copy.88), calls=%async_computation.3 | async-start | bytes 524288 | tf_op jit(solution)/shard_map/all_to_all | solution.py:28
  233.8 114.8 %all-reduce.7.cloned.1.call-start = ((), (), s32[]{:S(2)}) async-start(), calls=%async_computation.16 | async-start | bytes 524288 | tf_op jit(solution)/shard_map/psum | solution.py:164
  236.0 5.8 %copy-start.10 = (bf16[256,512]{0,1:T(8,128)(2,1)S(1)}, bf16[256,512]{0,1:T(8,128)(2,1)}, u32[]{:S(2)}) copy-start(bf16[256,512]{0,1:T(8,128)(2,1)} %copy.99) | copy-start | bytes 786436
  243.1 152.7 %reduce-scatter.13.cloned.1.call-start = ((), (), s32[]{:S(2)}) async-start(), calls=%async_computation.18 | async-start | bytes 2359296 | tf_op jit(solution)/shard_map/reduce_scatter | solution.py:39
  275.9 166.8 %reduce-scatter.9.cloned.1.call-start = ((), (), s32[]{:S(2)}) async-start(), calls=%async_computation.14 | async-start | bytes 2359296 | tf_op jit(solution)/shard_map/reduce_scatter | solution.py:39
  279.8 218.4 %copy-start.5 = (bf16[256,4,4,128]{0,3,2,1:T(8,128)(2,1)S(1)}, bf16[256,4,4,128]{0,3,2,1:T(8,128)(2,1)}, u32[]{:S(2)}) copy-start(bf16[256,4,4,128]{0,3,2,1:T(8,128)(2,1)} %copy-done.4) | copy-start | bytes 3145732
  279.8 215.2 %all-reduce.9.cloned.1.call-start = ((), (), s32[]{:S(2)}) async-start(), calls=%async_computation.17 | async-start | bytes 524288 | tf_op jit(solution)/shard_map/psum | solution.py:164
  348.7 169.0 %reduce-scatter.15.cloned.1.call-start = ((), (), s32[]{:S(2)}) async-start(), calls=%async_computation.19 | async-start | bytes 393216 | tf_op jit(solution)/shard_map/reduce_scatter | solution.py:40
  395.8 145.5 %reduce-scatter.11.cloned.1.call-start = ((), (), s32[]{:S(2)}) async-start(), calls=%async_computation.15 | async-start | bytes 393216 | tf_op jit(solution)/shard_map/reduce_scatter | solution.py:40
Sparse Core Ops, SparseCore 0:
  13.7 42.2 all-gather.12
  58.1 22.8 all-gather.8
  83.0 37.5 all-gather.14
  122.5 22.7 all-gather.10
  217.4 54.4 all-reduce.10
  274.7 73.9 all-reduce.6
  351.7 43.9 reduce-scatter.12
  398.8 43.7 reduce-scatter.8
  445.8 49.1 all-reduce.8
  498.2 19.4 reduce-scatter.14
  521.3 19.9 reduce-scatter.10
